TPU v7x, 128 devices: a whole 4x4x4 slice. The times are simulated.
128 devices in a mesh: sec: 2 (over x_hi), head: 4 (over x_lo, core), ctx: 16 (over z, y).
Axes of the slice: x: 4 (x_hi: 2, x_lo: 2; x = x_hi * 2 + x_lo), y: 4, z: 4, core: 2. Of those that a mesh axis runs over, the one named last changes fastest.
Arguments:
- proposal_rows: bfloat16 [512, 8192], P('sec', 'ctx'), may hold values from -400 to 400
- norm_gain: bfloat16 [8192], P('ctx'), may hold values from 0.25 to 1.75
- query_weight: bfloat16 [8192, 8192], P('ctx', ('sec', 'head')), may hold values from -0.0625 to 0.0625
- key_weight: bfloat16 [8192, 8, 128], P('ctx', ('sec', 'head')), may hold values from -0.25 to 0.25
- value_weight: bfloat16 [8192, 8, 128], P('ctx', ('sec', 'head')), may hold values from -0.0625 to 0.0625
- out_weight: bfloat16 [8192, 8192], P(('sec', 'head'), 'ctx'), may hold values from -0.0625 to 0.0625
- context_keys: bfloat16 [32768, 8, 128], P('ctx', ('sec', 'head')), may hold values from -256 to 256
- context_values: bfloat16 [32768, 8, 128], P('ctx', ('sec', 'head')), may hold values from -5 to 5
- prefix_lengths: int32 [32], replicated, may hold values from 2048 to 32768, as said below
- parents: int32 [512], replicated, may hold values from -1 to 510, as said below
Outputs:
- block_output: bfloat16 [512, 8192], P(('sec', 'head'), 'ctx')
Inputs may be any that keep to these rules, and one draw needn't show every extreme that they name: `parents`: token i = 16 p + s of particle p has parent -1 when s = 0, else 16 q + s - 1 for some particle q <= p. `prefix_lengths`: some particle sees the whole context.
All inputs are finite; a program needn't handle non-finite values.
Results may differ from a plain program's by a relative error of at most 0.015.
The roundings to bfloat16 on the way count: a program that leaves them out, or rounds other values in their place, can miss the bound.
Values may be sent and summed in bfloat16 or wider, within the bound.
No kernel may reach another device: no remote copies, remote signals or barrier semaphores. Data moves between devices by JAX's collectives and lax.ppermute only.
A program may use at most 192 MiB of HBM per device.

v0:
```python
import math
import jax
import jax.numpy as jnp
from jax import lax
from jax.sharding import PartitionSpec as P

D = 8192
PROPOSALS = 16
NEGATIVE = -1e30
EPSILON = 1e-05


def ancestry_columns(parents, column_offset, column_amount):
    total = parents.shape[0]
    index = jnp.arange(total, dtype=jnp.int32)
    step = jnp.logical_or(parents[:, None] == index[None, :], index[:, None] == index[None, :])
    reach = step.astype(jnp.bfloat16)
    for _ in range(3):
        reach = (jnp.dot(reach, reach, preferred_element_type=jnp.float32) > 0).astype(jnp.bfloat16)
    columns = lax.dynamic_slice_in_dim(reach, column_offset, column_amount, 1)
    return jnp.dot(reach, columns, preferred_element_type=jnp.float32) > 0


def body(
    proposal_rows,
    norm_gain,
    query_weight,
    key_weight,
    value_weight,
    out_weight,
    context_keys,
    context_values,
    prefix_lengths,
    parents,
):
    gathered = lax.all_gather(proposal_rows, "sec", axis=0, tiled=True)
    gathered_wide = gathered.astype(jnp.float32)
    total_rows = gathered.shape[0]
    squares = jnp.sum(gathered_wide * gathered_wide, axis=1)
    scaled = (gathered_wide * norm_gain.astype(jnp.float32)[None, :]).astype(jnp.bfloat16)
    query_width = query_weight.shape[1]
    head_size = key_weight.shape[2]
    groups = query_width // head_size
    joined = jnp.concatenate([query_weight, key_weight[:, 0, :], value_weight[:, 0, :]], axis=1)
    partial_value = jnp.dot(scaled, joined, preferred_element_type=jnp.float32)
    proj_width = partial_value.shape[1]
    lane = jnp.arange(128, dtype=jnp.int32)
    square_block = jnp.where(lane[None, :] == 0, squares[:, None], 0.0)
    packed = jnp.concatenate([partial_value, square_block], axis=1)
    reduced = lax.psum_scatter(packed, "ctx", scatter_dimension=0, tiled=True)
    row_share = reduced.shape[0]
    inverse = lax.rsqrt(reduced[:, proj_width] / D + EPSILON)[:, None]
    settled = reduced[:, :proj_width] * inverse
    own_queries = settled[:, :query_width].astype(jnp.bfloat16)
    tree_keys = settled[:, query_width : query_width + head_size].astype(jnp.bfloat16)
    tree_vals = settled[:, query_width + head_size :].astype(jnp.bfloat16)
    queries = lax.all_gather(own_queries, "ctx", axis=0, tiled=True)
    position = lax.axis_index("ctx")
    keys = context_keys[:, 0, :]
    vals = context_values[:, 0, :]
    span = keys.shape[0]
    factor = 1.0 / math.sqrt(head_size)
    grouped = queries.reshape(total_rows, groups, head_size)
    lengths_rows = jnp.repeat(prefix_lengths, PROPOSALS)
    positions = position * span + jnp.arange(span, dtype=jnp.int32)
    visible = (positions[None, :] < lengths_rows[:, None])[:, None, :]
    scores = jnp.einsum("rgd,td->rgt", grouped, keys, preferred_element_type=jnp.float32) * factor
    tree_visible = ancestry_columns(parents, position * row_share, row_share)[:, None, :]
    tree_scores = (
        jnp.einsum("rgd,td->rgt", grouped, tree_keys, preferred_element_type=jnp.float32) * factor
    )
    local_high = jnp.maximum(
        jnp.max(jnp.where(visible, scores, NEGATIVE), axis=2),
        jnp.max(jnp.where(tree_visible, tree_scores, NEGATIVE), axis=2),
    )
    highest = lax.pmax(local_high, "ctx")
    weights = jnp.where(visible, jnp.exp(scores - highest[:, :, None]), 0.0)
    tree_weights = jnp.where(tree_visible, jnp.exp(tree_scores - highest[:, :, None]), 0.0)
    weight_sum = jnp.sum(weights, axis=2) + jnp.sum(tree_weights, axis=2)
    summed = jnp.einsum(
        "rgt,td->rgd", weights.astype(jnp.bfloat16), vals, preferred_element_type=jnp.float32
    ) + jnp.einsum(
        "rgt,td->rgd",
        tree_weights.astype(jnp.bfloat16),
        tree_vals,
        preferred_element_type=jnp.float32,
    )
    sum_block = jnp.concatenate(
        [weight_sum, jnp.zeros((total_rows, 128 - groups), jnp.float32)], axis=1
    )
    packed_attn = jnp.concatenate([summed.reshape(total_rows, query_width), sum_block], axis=1)
    merged = lax.psum_scatter(packed_attn, "ctx", scatter_dimension=0, tiled=True)
    own_attended = (
        (
            merged[:, :query_width].reshape(row_share, groups, head_size)
            / merged[:, query_width : query_width + groups][:, :, None]
        )
        .reshape(row_share, query_width)
        .astype(jnp.bfloat16)
    )
    attended = lax.all_gather(own_attended, "ctx", axis=0, tiled=True)
    return lax.psum_scatter(
        jnp.dot(attended, out_weight, preferred_element_type=jnp.float32).astype(jnp.bfloat16),
        ("sec", "head"),
        scatter_dimension=0,
        tiled=True,
    )


def solution(mesh):
    placed = (
        P("sec", "ctx"),
        P("ctx"),
        P("ctx", ("sec", "head")),
        P("ctx", ("sec", "head"), None),
        P("ctx", ("sec", "head"), None),
        P(("sec", "head"), "ctx"),
        P("ctx", ("sec", "head"), None),
        P("ctx", ("sec", "head"), None),
        P(),
        P(),
    )
    return jax.shard_map(
        body, mesh=mesh, in_specs=placed, out_specs=P(("sec", "head"), "ctx"), check_vma=False
    )
```

profile of v0, /device:TPU:0, one launch (start us, length us, event | category | flops | bytes accessed | tf_op | source)
XLA Modules:
  0.0 426.5 jit_solution(10706751456148544928)
XLA Ops:
  6.5 10.5 %all_gather.9 = bf16[512,512]{1,0:T(8,128)(2,1)S(1)} all-gather(bf16[256,512]{1,0:T(8,128)(2,1)} %param.10), channel_id=1, replica_groups=mesh['sec'=2,'head'=4,'ctx'=16] {'sec'}, dimensions={0}, use_global_device_ids=true | all-gather | bytes 786432 | tf_op jit(solution)/shard_map/all_gather | solution.py:36
  17.0 0.7 convert_element_type.29
  18.0 2.2 fusion.5
  20.3 1.8 pad_maximum_fusion
  22.1 79.1 %reduce-scatter.6.cloned.1.call-done = f32[32,1408]{1,0:T(8,128)} async-done(((f32[512,1408]{1,0:T(8,128)}), f32[32,1408]{1,0:T(8,128)}) %reduce-scatter.6.cloned.1.call-update) | async-done | bytes 180240 | tf_op jit(solution)/shard_map/reduce_scatter | solution.py:50
  101.3 0.8 fusion.37
  102.1 1.0 fusion.34
  104.7 1.1 convolution_compare_fusion
  106.3 0.7 broadcast_compare_fusion
  106.9 38.8 %all-gather.3.cloned.1.call-done = bf16[512,1024]{1,0:T(8,128)(2,1)} async-done(((bf16[32,1024]{1,0:T(8,128)(2,1)}), bf16[512,1024]{1,0:T(8,128)(2,1)}) %all-gather.3.cloned.1.call-update) | async-done | bytes 1048592 | tf_op jit(solution)/shard_map/all_gather | solution.py:57
  145.7 1.7 select_reduce_fusion.1
  147.4 15.1 %select_reduce_fusion = (f32[512,8]{0,1:T(8,128)S(1)}, f32[512,8,2048]{2,0,1:T(8,128)}) fusion(pred[512,2048]{1,0:T(8,128)(4,1)S(1)} %broadcast_compare_fusion, bf16[2048,1,128]{2,0,1:T(8,128)(2,1)S(1)} %copy-done.1, bf16[512,1024]{1,0:T(8,128)(2,1)} %all-gather.3.cloned.1.call-done), kind=kOutput, calls=%fused_computation.1 | convolution fusion | flops 2172645376 | bytes 36192256 | tf_op jit(solution)/shard_map/rgd,td->rgt/dot_general | solution.py:67
  162.5 72.1 %pmax.7 = f32[512,8]{0,1:T(8,128)S(1)} all-reduce(f32[512,8]{0,1:T(8,128)S(1)} %max.5), channel_id=1, replica_groups=mesh['sec'=2,'head'=4,'ctx'=16] {'ctx'}, use_global_device_ids=true, to_apply=%region_4.5 | all-reduce | flops 4096 | bytes 32768 | tf_op jit(solution)/shard_map/pmax | solution.py:76
  234.6 15.2 %fusion = f32[512,8]{0,1:T(8,128)S(1)} fusion(f32[512,8,2048]{2,0,1:T(8,128)} %get-tuple-element.6, f32[512,8]{0,1:T(8,128)S(1)} %pmax.7, pred[512,2048]{1,0:T(8,128)(4,1)S(1)} %broadcast_compare_fusion), kind=kLoop, calls=%fused_computation.2 | loop fusion | flops 33550336 | bytes 34635776 | tf_op jit(solution)/shard_map/reduce_sum | solution.py:79
  249.8 15.4 %fusion.2 = f32[512,8,128]{0,2,1:T(8,128)} fusion(f32[512,8,2048]{2,0,1:T(8,128)} %get-tuple-element.6, f32[512,8]{0,1:T(8,128)S(1)} %pmax.7, pred[512,2048]{1,0:T(8,128)(4,1)S(1)} %broadcast_compare_fusion, bf16[2048,1,128]{2,0,1:T(8,128)(2,1)} %param.17), kind=kOutput, calls=%fused_computation.4 | convolution fusion | flops 2181038080 | bytes 37240832 | tf_op jit(solution)/shard_map/rgt,td->rgd/dot_general | solution.py:80
  265.3 2.1 convolution_add_fusion
  267.7 2.0 copy.25
  269.7 72.2 %reduce-scatter.10.cloned.1.call-done = f32[32,1152]{1,0:T(8,128)} async-done(((f32[512,1152]{1,0:T(8,128)}), f32[32,1152]{1,0:T(8,128)}) %reduce-scatter.10.cloned.1.call-update) | async-done | bytes 147472
  341.9 0.9 slice.36
  343.0 0.7 slice.37
  343.8 0.8 copy.21
  344.7 42.0 %all-gather.5.cloned.1.call-done = bf16[512,1024]{1,0:T(8,128)(2,1)} async-done(((bf16[32,1024]{1,0:T(8,128)(2,1)}), bf16[512,1024]{1,0:T(8,128)(2,1)}) %all-gather.5.cloned.1.call-update) | async-done | bytes 1048592 | tf_op jit(solution)/shard_map/all_gather | solution.py:101
  386.6 2.8 convolution_convert_fusion
  389.4 30.6 %reduce-scatter.8.cloned.1.call-done = bf16[64,512]{1,0:T(8,128)(2,1)} async-done(((bf16[512,512]{1,0:T(8,128)(2,1)}), bf16[64,512]{1,0:T(8,128)(2,1)}) %reduce-scatter.8.cloned.1.call-update) | async-done | bytes 65552 | tf_op jit(solution)/shard_map/reduce_scatter | solution.py:102
  (36 shorter events, 3.2 us)
Async XLA Ops:
  6.5 380.1 %copy-start = (bf16[1024,512]{1,0:T(8,128)(2,1)S(1)}, bf16[1024,512]{1,0:T(8,128)(2,1)}, u32[]{:S(2)}) copy-start(bf16[1024,512]{1,0:T(8,128)(2,1)} %param.15) | copy-start | bytes 3145732
  6.5 94.7 %reduce-scatter.6.cloned.1.call-start = ((), (), s32[]{:S(2)}) async-start(), calls=%async_computation.3 | async-start | bytes 3063808 | tf_op jit(solution)/shard_map/reduce_scatter | solution.py:50
  22.1 81.8 %copy-start.2 = (s32[32]{0:T(128)S(1)}, s32[32]{0:T(128)}, u32[]{:S(2)}) copy-start(s32[32]{0:T(128)} %param.18) | copy-start | bytes 388
  22.1 82.0 %copy-start.3 = (s32[512]{0:T(512)S(1)}, s32[512]{0:T(512)}, u32[]{:S(2)}) copy-start(s32[512]{0:T(512)} %param.19) | copy-start | bytes 6148
  22.1 123.6 %all-gather.3.cloned.1.call-start = ((), (), s32[]{:S(2)}) async-start(), calls=%async_computation.4 | async-start | bytes 1114112 | tf_op jit(solution)/shard_map/all_gather | solution.py:57
  103.8 238.1 %reduce-scatter.10.cloned.1.call-start = ((), (), s32[]{:S(2)}) async-start(), calls=%async_computation.7 | async-start | bytes 2506752
  104.7 42.7 %copy-start.1 = (bf16[2048,1,128]{2,0,1:T(8,128)(2,1)S(1)}, bf16[2048,1,128]{2,0,1:T(8,128)(2,1)}, u32[]{:S(2)}) copy-start(bf16[2048,1,128]{2,0,1:T(8,128)(2,1)} %param.16) | copy-start | bytes 1572868
  269.7 117.0 %all-gather.5.cloned.1.call-start = ((), (), s32[]{:S(2)}) async-start(), calls=%async_computation.5 | async-start | bytes 1114112 | tf_op jit(solution)/shard_map/all_gather | solution.py:101
  344.6 75.4 %reduce-scatter.8.cloned.1.call-start = ((), (), s32[]{:S(2)}) async-start(), calls=%async_computation.6 | async-start | bytes 589824 | tf_op jit(solution)/shard_map/reduce_scatter | solution.py:102
Sparse Core Ops, SparseCore 0:
  22.2 79.0 reduce-scatter.5
  103.9 41.7 all-gather.2
  269.8 72.0 reduce-scatter.9
  344.7 41.8 all-gather.4
  389.5 30.4 reduce-scatter.7
where the time goes:
time: 427 us
  waiting for transfers between devices  263 us (62%)
  blocking collectives  82.6 us (19%)
  matrix products  41.4 us (10%)
  other arithmetic  20.8 us (5%)
  between operations  13.3 us (3%)
  local copies, waits for them, and re-layouts  5.52 us (1%)
    reduce_scatter x1, waiting for transfers between devices, body(): reduced = lax.psum_scatter(packed, 'ctx', scatter_dimension=0, tiled=True)  79.1 us
    unnamed x6, waiting for transfers between devices  72.2 us
    pmax x1, blocking collectives, body(): highest = lax.pmax(local_high, 'ctx')  72.1 us
    all_gather x1, waiting for transfers between devices, body(): attended = lax.all_gather(own_attended, 'ctx', axis=0, tiled=True)  42 us
    all_gather x1, waiting for transfers between devices, body(): queries = lax.all_gather(own_queries, 'ctx', axis=0, tiled=True)  38.8 us
    reduce_scatter x1, waiting for transfers between devices, body(): lax.psum_scatter(jnp.dot(attended, out_weight, preferred_element_type=jnp...  30.6 us
    dot_general x1, matrix products, body(): jnp.einsum('rgt,td->rgd', weights.astype(jnp.bfloat16), vals, preferred_e...  15.4 us
    reduce_sum x2, other arithmetic, body(): weight_sum = jnp.sum(weights, axis=2) + jnp.sum(tree_weights, axis=2)  15.3 us
  transfers between devices with their start and end apart: 5, of which 5 were waited for; matrix products, arithmetic and copies ran while one was open for 1% of the time, Pallas kernels for 0%

commit v1 on v0

--- a/solution.py
+++ b/solution.py
@@ -98,7 +98,10 @@
         .reshape(row_share, query_width)
         .astype(jnp.bfloat16)
     )
-    attended = lax.all_gather(own_attended, "ctx", axis=0, tiled=True)
+    n_lanes = lax.axis_size("ctx")
+    table = [n_lanes if u == 0 else 1 for u in range(own_attended.ndim)]
+    part_next = jnp.tile(own_attended, table)
+    attended = lax.all_to_all(part_next, axis_name="ctx", concat_axis=0, tiled=True, split_axis=0)
     return lax.psum_scatter(
         jnp.dot(attended, out_weight, preferred_element_type=jnp.float32).astype(jnp.bfloat16),
         ("sec", "head"),

time: 427 us -> 402 us (0.941)
  waiting for transfers between devices: 263 us -> 219 us
  blocking collectives: 82.6 us -> 103 us
    all_gather x1 -> x0, waiting for transfers between devices: 42 us -> none  [body(): attended = lax.all_gather(own_attended, 'ctx', axis=0, tiled=True)]
    all_to_all x0 -> x1, blocking collectives: none -> 20.1 us  [body(): lax.all_to_all(part_next, axis_name='ctx', concat_axis=0, tiled=True, spl...]
    unnamed x6 -> x5, waiting for transfers between devices: 72.2 us -> 72.2 us
  transfers between devices with their start and end apart: 5 -> 4, of which waited for: 5 -> 4; matrix products, arithmetic and copies ran while one was open for 1% -> 1% of each run, Pallas kernels for 0% -> 0%
where the time goes in v1:
time: 402 us; the launch traced here: 401 us
  waiting for transfers between devices  219 us (54%)
  blocking collectives  103 us (26%)
  matrix products  40.2 us (10%)
  other arithmetic  20.8 us (5%)
  between operations  13.3 us (3%)
  local copies, waits for them, and re-layouts  5 us (1%)
    reduce_scatter x1, waiting for transfers between devices, body(): reduced = lax.psum_scatter(packed, 'ctx', scatter_dimension=0, tiled=True)  79.1 us
    unnamed x5, waiting for transfers between devices  72.2 us
    pmax x1, blocking collectives, body(): highest = lax.pmax(local_high, 'ctx')  72.1 us
    all_gather x1, waiting for transfers between devices, body(): queries = lax.all_gather(own_queries, 'ctx', axis=0, tiled=True)  38.8 us
    reduce_scatter x1, waiting for transfers between devices, body(): lax.psum_scatter(jnp.dot(attended, out_weight, preferred_element_type=jnp...  28.7 us
    all_to_all x1, blocking collectives, body(): lax.all_to_all(part_next, axis_name='ctx', concat_axis=0, tiled=True, spl...  20.1 us
    dot_general x1, matrix products, body(): jnp.einsum('rgt,td->rgd', weights.astype(jnp.bfloat16), vals, preferred_e...  15.4 us
    reduce_sum x2, other arithmetic, body(): weight_sum = jnp.sum(weights, axis=2) + jnp.sum(tree_weights, axis=2)  15.3 us
  transfers between devices with their start and end apart: 4, of which 4 were waited for; matrix products, arithmetic and copies ran while one was open for 1% of the time, Pallas kernels for 0%

profile of v1, /device:TPU:0, one launch (start us, length us, event | category | flops | bytes accessed | tf_op | source)
XLA Modules:
  0.0 400.9 jit_solution(6179837839018597343)
XLA Ops:
  6.5 10.5 %all_gather.6 = bf16[512,512]{1,0:T(8,128)(2,1)S(1)} all-gather(bf16[256,512]{1,0:T(8,128)(2,1)} %param.10), channel_id=1, replica_groups=mesh['sec'=2,'head'=4,'ctx'=16] {'sec'}, dimensions={0}, use_global_device_ids=true | all-gather | bytes 786432 | tf_op jit(solution)/shard_map/all_gather | solution.py:36
  17.0 0.7 convert_element_type.29
  18.0 2.2 fusion.5
  20.3 1.8 pad_maximum_fusion
  22.1 79.1 %reduce-scatter.6.cloned.1.call-done = f32[32,1408]{1,0:T(8,128)} async-done(((f32[512,1408]{1,0:T(8,128)}), f32[32,1408]{1,0:T(8,128)}) %reduce-scatter.6.cloned.1.call-update) | async-done | bytes 180240 | tf_op jit(solution)/shard_map/reduce_scatter | solution.py:50
  101.3 0.8 fusion.37
  102.1 1.0 fusion.34
  104.1 0.6 convolution_compare_fusion.2
  104.7 1.1 convolution_compare_fusion
  106.3 0.7 broadcast_compare_fusion
  106.9 38.8 %all-gather.2.cloned.1.call-done = bf16[512,1024]{1,0:T(8,128)(2,1)} async-done(((bf16[32,1024]{1,0:T(8,128)(2,1)}), bf16[512,1024]{1,0:T(8,128)(2,1)}) %all-gather.2.cloned.1.call-update) | async-done | bytes 1048592 | tf_op jit(solution)/shard_map/all_gather | solution.py:57
  145.7 1.7 select_reduce_fusion.1
  147.4 15.1 %select_reduce_fusion = (f32[512,8]{0,1:T(8,128)S(1)}, f32[512,8,2048]{2,0,1:T(8,128)}) fusion(pred[512,2048]{1,0:T(8,128)(4,1)S(1)} %broadcast_compare_fusion, bf16[2048,1,128]{2,0,1:T(8,128)(2,1)S(1)} %copy-done.1, bf16[512,1024]{1,0:T(8,128)(2,1)} %all-gather.2.cloned.1.call-done), kind=kOutput, calls=%fused_computation.1 | convolution fusion | flops 2172645376 | bytes 36192256 | tf_op jit(solution)/shard_map/rgd,td->rgt/dot_general | solution.py:67
  162.5 72.1 %pmax.7 = f32[512,8]{0,1:T(8,128)S(1)} all-reduce(f32[512,8]{0,1:T(8,128)S(1)} %max.5), channel_id=1, replica_groups=mesh['sec'=2,'head'=4,'ctx'=16] {'ctx'}, use_global_device_ids=true, to_apply=%region_4.5 | all-reduce | flops 4096 | bytes 32768 | tf_op jit(solution)/shard_map/pmax | solution.py:76
  234.6 15.2 %fusion = f32[512,8]{0,1:T(8,128)S(1)} fusion(f32[512,8,2048]{2,0,1:T(8,128)} %get-tuple-element.6, f32[512,8]{0,1:T(8,128)S(1)} %pmax.7, pred[512,2048]{1,0:T(8,128)(4,1)S(1)} %broadcast_compare_fusion), kind=kLoop, calls=%fused_computation.2 | loop fusion | flops 33550336 | bytes 34635776 | tf_op jit(solution)/shard_map/reduce_sum | solution.py:79
  249.8 15.4 %fusion.2 = f32[512,8,128]{0,2,1:T(8,128)} fusion(f32[512,8,2048]{2,0,1:T(8,128)} %get-tuple-element.6, f32[512,8]{0,1:T(8,128)S(1)} %pmax.7, pred[512,2048]{1,0:T(8,128)(4,1)S(1)} %broadcast_compare_fusion, bf16[2048,1,128]{2,0,1:T(8,128)(2,1)} %param.17), kind=kOutput, calls=%fused_computation.4 | convolution fusion | flops 2181038080 | bytes 37240832 | tf_op jit(solution)/shard_map/rgt,td->rgd/dot_general | solution.py:80
  265.3 2.1 convolution_add_fusion
  267.7 2.0 copy.27
  269.7 72.2 %reduce-scatter.10.cloned.1.call-done = f32[32,1152]{1,0:T(8,128)} async-done(((f32[512,1152]{1,0:T(8,128)}), f32[32,1152]{1,0:T(8,128)}) %reduce-scatter.10.cloned.1.call-update) | async-done | bytes 147472
  341.9 0.9 slice.36
  343.0 0.7 slice.37
  344.1 20.1 %all_to_all.9 = bf16[16,32,1024]{2,1,0:T(8,128)(2,1)S(1)} all-to-all(bf16[16,32,1024]{2,1,0:T(8,128)(2,1)S(1)} %tile.2), channel_id=1, replica_groups=mesh['sec'=2,'head'=4,'ctx'=16] {'ctx'}, dimensions={0} | all-to-all | bytes 2097152 | tf_op jit(solution)/shard_map/all_to_all | solution.py:104
  364.2 1.5 convolution_convert_fusion
  365.7 28.7 %reduce-scatter.8.cloned.1.call-done = bf16[64,512]{1,0:T(8,128)(2,1)} async-done(((bf16[512,512]{1,0:T(8,128)(2,1)}), bf16[64,512]{1,0:T(8,128)(2,1)}) %reduce-scatter.8.cloned.1.call-update) | async-done | bytes 65552 | tf_op jit(solution)/shard_map/reduce_scatter | solution.py:105
  (35 shorter events, 2.7 us)
Async XLA Ops:
  6.5 357.6 %copy-start = (bf16[1024,512]{1,0:T(8,128)(2,1)S(1)}, bf16[1024,512]{1,0:T(8,128)(2,1)}, u32[]{:S(2)}) copy-start(bf16[1024,512]{1,0:T(8,128)(2,1)} %param.15) | copy-start | bytes 3145732
  6.5 94.7 %reduce-scatter.6.cloned.1.call-start = ((), (), s32[]{:S(2)}) async-start(), calls=%async_computation.4 | async-start | bytes 3063808 | tf_op jit(solution)/shard_map/reduce_scatter | solution.py:50
  22.1 81.8 %copy-start.2 = (s32[32]{0:T(128)S(1)}, s32[32]{0:T(128)}, u32[]{:S(2)}) copy-start(s32[32]{0:T(128)} %param.18) | copy-start | bytes 388
  22.1 82.0 %copy-start.3 = (s32[512]{0:T(512)S(1)}, s32[512]{0:T(512)}, u32[]{:S(2)}) copy-start(s32[512]{0:T(512)} %param.19) | copy-start | bytes 6148
  22.1 123.6 %all-gather.2.cloned.1.call-start = ((), (), s32[]{:S(2)}) async-start(), calls=%async_computation.5 | async-start | bytes 1114112 | tf_op jit(solution)/shard_map/all_gather | solution.py:57
  103.8 238.1 %reduce-scatter.10.cloned.1.call-start = ((), (), s32[]{:S(2)}) async-start(), calls=%async_computation.7 | async-start | bytes 2506752
  104.7 42.7 %copy-start.1 = (bf16[2048,1,128]{2,0,1:T(8,128)(2,1)S(1)}, bf16[2048,1,128]{2,0,1:T(8,128)(2,1)}, u32[]{:S(2)}) copy-start(bf16[2048,1,128]{2,0,1:T(8,128)(2,1)} %param.16) | copy-start | bytes 1572868
  269.7 124.7 %reduce-scatter.8.cloned.1.call-start = ((), (), s32[]{:S(2)}) async-start(), calls=%async_computation.6 | async-start | bytes 589824 | tf_op jit(solution)/shard_map/reduce_scatter | solution.py:105
Sparse Core Ops, SparseCore 0:
  22.2 79.0 reduce-scatter.5
  103.9 41.7 all-gather.1
  269.8 72.0 reduce-scatter.9
  365.8 28.5 reduce-scatter.7
